TPU v7x, 512 devices: a whole 4x8x8 slice. The times are simulated.
512 devices in a mesh: sub: 128 (over z, y, core), harm: 4 (over x).
Axes of the slice: x: 4, y: 8, z: 8, core: 2. Of those that a mesh axis runs over, the one named last changes fastest.
Arguments:
- lengths: int32 [384], P('sub'), may hold values from 128 to 1024, as said below
- owners: int32 [384, 1], P('sub'), may hold values from 0 to 127, as said below
- front_inverse: bfloat16 [384, 1024, 1024], P('sub', 'harm'), may hold values from -0.1875 to 0.1875
- coupling: bfloat16 [384, 1024, 768], P('sub', 'harm'), may hold values from -0.1875 to 0.1875
- stiffness: bfloat16 [384, 768, 768], P('sub', 'harm'), may hold values from -0.21875 to 0.21875
- displacement: bfloat16 [128, 32, 768], P('sub', 'harm'), may hold values from -6 to 6
- forcing: float32 [128, 32, 768], P('sub', 'harm'), may hold values from -6 to 6
- lumped_mass: float32 [128, 768], P('sub'), may hold values from 0.2 to 2
- damping: float32 [128, 768], P('sub'), may hold values from 0.1 to 1.5
Outputs:
- interior: bfloat16 [384, 32, 1024], P('sub', None, 'harm')
- residual: float32 [128, 32, 768], P('sub', 'harm')
- modes: bfloat16 [384, 1024, 768], P('sub', 'harm')
Inputs may be any that keep to these rules, and one draw needn't show every extreme that they name: `lengths`: live interior front rows of each substructure, which are its first rows; some substructure has all 1024. `owners`: substructure k lies on sub index k // 3; on every sub index d, the first 2 of its 3 substructures are attached to block (d + 64) mod 128, the third to a block of uneven popularity; every interface block has at least one substructure.
All inputs are finite; a program needn't handle non-finite values.
Results may differ from a plain program's by a relative error of at most 0.008.
Values may be sent and summed in bfloat16 or wider, within the bound.
No kernel may reach another device: no remote copies, remote signals or barrier semaphores. Data moves between devices by JAX's collectives and lax.ppermute only.
A program may use at most 64 MiB of HBM per device.

v0:
```python
import jax
import jax.numpy as jnp
from jax import lax
from jax.sharding import Mesh
from jax.sharding import PartitionSpec as P

SUB = ("sub_0", "sub_1", "sub_2")
PLANE = ("sub_0", "sub_1")
PAIR = ("sub_2", "harm")


def copy_for_each(x, axis):
    length = lax.axis_size(axis)
    return lax.all_to_all(jnp.broadcast_to(x[None], (length, *x.shape)), axis, 0, 0, tiled=True)


def joined_along(tiles, dim):
    tiles = jnp.moveaxis(tiles, 0, dim)
    shape = tiles.shape
    return tiles.reshape(*shape[:dim], shape[dim] * shape[dim + 1], *shape[dim + 2 :])


def whole_of(x, axes, dim):
    far, near = axes
    tiles = copy_for_each(copy_for_each(x, far), near)
    return joined_along(tiles.swapaxes(0, 1).reshape(-1, *x.shape), dim)


def collect(x, axis, dim):
    tiles = copy_for_each(x, axis)
    return joined_along(tiles, dim)


def in_blocks(x, dim, length):
    shape = x.shape
    tiles = x.reshape(*shape[:dim], length, shape[dim] // length, *shape[dim + 1 :])
    return jnp.moveaxis(tiles, dim, 0)


def sent_and_summed(x, axis, dim):
    tiles = in_blocks(x, dim, lax.axis_size(axis))
    arrived = lax.all_to_all(tiles, axis, split_axis=0, concat_axis=0, tiled=True)
    return arrived.astype(jnp.float32).sum(axis=0)


def body(
    lengths, owners, front_inverse, coupling, stiffness, displacement, forcing, lumped_mass, damping
):
    nharm = lax.axis_size("harm")
    harm_idx = lax.axis_index("harm")
    front_q = coupling.shape[1]
    width = coupling.shape[2]
    width_q = stiffness.shape[1]
    nown = lax.axis_size(SUB)
    own_rows = harm_idx * front_q + jnp.arange(front_q, dtype=jnp.int32)
    live_rows = own_rows[None, :] < lengths[:, None]
    masked = jnp.where(live_rows[:, :, None], coupling, jnp.zeros_like(coupling))
    piece = lax.all_gather(coupling, "harm", axis=1, tiled=True)
    live_cols = jnp.arange(nharm * front_q, dtype=jnp.int32)[None, :] < lengths[:, None]
    front_live = jnp.where(live_cols[:, None, :], front_inverse, jnp.zeros_like(front_inverse))
    modes = jnp.einsum(
        "sfg,sgn->sfn", front_live, piece, preferred_element_type=jnp.float32
    ).astype(jnp.bfloat16)
    nplane = lax.axis_size(PLANE)
    rows_q = displacement.shape[1]
    core = lax.axis_index("sub_2")
    near = (lax.axis_index(SUB) + nown // 2) % nown
    third = owners[2, 0]
    other = lax.ppermute(owners[2:3, 0], "sub_2", [(0, 1), (1, 0)])[0]
    plane = copy_for_each(displacement[0], PLANE)
    lent = lax.ppermute(
        lax.dynamic_index_in_dim(plane, other // 2, 0, keepdims=False), "sub_2", [(0, 1), (1, 0)]
    )
    here = lax.dynamic_index_in_dim(plane, third // 2, 0, keepdims=False)
    picked = jnp.stack(
        [
            lax.dynamic_index_in_dim(plane, near // 2, 0, keepdims=False),
            jnp.where(third % 2 == core, here, lent),
        ]
    )
    own_pair = collect(picked, "harm", 1)
    own_disp = jnp.stack([own_pair[0], own_pair[0], own_pair[1]])
    inner = -jnp.einsum("sfn,shn->shf", modes, own_disp, preferred_element_type=jnp.float32)
    interior = jnp.where(live_rows[:, None, :], inner, jnp.float32(0.0)).astype(jnp.bfloat16)
    disp_cols = lax.dynamic_slice_in_dim(own_disp, harm_idx * width_q, width_q, 2)
    contrib = jnp.einsum("shf,sfn->shn", interior, masked, preferred_element_type=jnp.float32)
    contrib = contrib + jnp.einsum(
        "shj,sjn->shn", disp_cols, stiffness, preferred_element_type=jnp.float32
    )
    near_c = (contrib[0] + contrib[1]).reshape(nharm, rows_q, width)
    third_c = contrib[2].reshape(nharm, rows_q, width)
    zero_rows = jnp.zeros_like(near_c)
    send = jnp.stack(
        [
            jnp.stack(
                [
                    jnp.where(peer_core == core, near_c, zero_rows),
                    jnp.where(third % 2 == peer_core, third_c, zero_rows),
                ],
                axis=1,
            )
            for peer_core in range(2)
        ]
    )
    came = lax.all_to_all(
        send.reshape(2 * nharm, 2, rows_q, width).astype(jnp.bfloat16), PAIR, 0, 0, tiled=True
    ).astype(jnp.float32)
    came = came.reshape(2, nharm, 2, rows_q, width).sum(axis=1)
    mine = jnp.where(core == 0, came[0], came[1])
    theirs = jnp.where(core == 0, came[1], came[0])
    near_part = mine[0]
    third_part = mine[1]
    other_part = theirs[1]
    slots = jnp.arange(nplane, dtype=jnp.int32)[:, None, None]
    dense = (
        jnp.where(slots == near // 2, near_part, jnp.float32(0.0))
        + jnp.where((slots == third // 2) & (third % 2 == core), third_part, jnp.float32(0.0))
        + jnp.where((slots == other // 2) & (other % 2 == core), other_part, jnp.float32(0.0))
    )
    arrived = lax.all_to_all(
        dense.astype(jnp.bfloat16), PLANE, split_axis=0, concat_axis=0, tiled=True
    ).astype(jnp.float32)
    gathered = jnp.sum(arrived, axis=0, keepdims=True)
    rows_q = displacement.shape[1]
    pairs_all = rows_q * nharm // 2
    rows = harm_idx * rows_q + jnp.arange(rows_q, dtype=jnp.int32)
    pair = (rows // 2).astype(jnp.float32)
    parity = (rows % 2).astype(jnp.float32)
    freq = 1.5 * (pair + 1.0) / pairs_all
    sign = 1.0 - 2.0 * parity
    disp = displacement.astype(jnp.float32)
    partner = disp.reshape(1, rows_q // 2, 2, width)[:, :, ::-1, :].reshape(1, rows_q, width)
    residual = (
        gathered
        - (freq * freq)[None, :, None] * lumped_mass[:, None, :] * disp
        + (sign * freq)[None, :, None] * damping[:, None, :] * partner
        - forcing
    )
    return (interior, residual, modes)


def solution(mesh):
    split = Mesh(
        mesh.devices.reshape(8, 8, 2, mesh.shape["harm"]), ("sub_0", "sub_1", "sub_2", "harm")
    )
    placed = (
        P(SUB),
        P(SUB, None),
        P(SUB, "harm", None),
        P(SUB, "harm", None),
        P(SUB, "harm", None),
        P(SUB, "harm", None),
        P(SUB, "harm", None),
        P(SUB, None),
        P(SUB, None),
    )
    return jax.shard_map(
        body,
        mesh=split,
        in_specs=placed,
        out_specs=(P(SUB, None, "harm"), P(SUB, "harm", None), P(SUB, "harm", None)),
        check_vma=False,
    )
```

profile of v0, /device:TPU:8, one launch (start us, length us, event | category | flops | bytes accessed | tf_op | source)
XLA Modules:
  0.0 136.1 jit_solution(10824814379573062923)
XLA Ops:
  7.2 0.7 all-gather.2.cloned.1.call-update
  7.9 1.6 %broadcast_in_dim.101 = bf16[64,8,768]{2,1,0:T(8,128)(2,1)} broadcast(bf16[8,768]{1,0:T(8,128)(2,1)} %bitcast.58), dimensions={1,2} | broadcast | bytes 798720 | tf_op jit(solution)/shard_map/broadcast_in_dim | solution.py:14
  9.6 16.6 %all-to-all-start = ((bf16[64,8,768]{2,1,0:T(8,128)(2,1)}), bf16[64,8,768]{2,1,0:T(8,128)(2,1)S(1)}, u32[]{:S(2)}, u32[]{:S(2)}) async-start(bf16[64,8,768]{2,1,0:T(8,128)(2,1)} %broadcast_in_dim.101), calls=%async_computation | async-start | bytes 1572864 | tf_op jit(solution)/shard_map/all_to_all | solution.py:14
  26.2 0.6 slice.46
  26.8 1.9 %collective-permute-start = (s32[1]{0:T(128)}, s32[1]{0:T(128)}, u32[]{:S(2)}, u32[]{:S(2)}) collective-permute-start(s32[1]{0:T(128)} %bitcast.3), channel_id=1, source_target_pairs={{0,4},{4,0},{1,5},{5,1},{2,6},{6,2},{3,7},{7,3},{8,12},{12,8},{9,1... | collective-permute-start | bytes 20 | tf_op jit(solution)/shard_map/ppermute | solution.py:69
  28.8 1.1 collective-permute-done
  32.4 17.7 %all-to-all-done = bf16[64,8,768]{2,1,0:T(8,128)(2,1)S(1)} async-done(((bf16[64,8,768]{2,1,0:T(8,128)(2,1)}), bf16[64,8,768]{2,1,0:T(8,128)(2,1)S(1)}, u32[]{:S(2)}, u32[]{:S(2)}) %all-to-all-start) | async-done | bytes 786464 | tf_op jit(solution)/shard_map/all_to_all | solution.py:14
  50.1 1.9 %collective-permute-start.1 = (bf16[8,768]{1,0:T(8,128)(2,1)S(1)}, bf16[8,768]{1,0:T(8,128)(2,1)S(1)}, u32[]{:S(2)}, u32[]{:S(2)}) collective-permute-start(bf16[8,768]{1,0:T(8,128)(2,1)S(1)} %get-tuple-element.4), channel_id=1, source_target_pairs={{0,4},{4,0},{1,5},{5,1},{2,6},{6,2},{3,7},{7,3},{8,12},{12,8},{9,1... | collective-permute-start | bytes 36872 | tf_op jit(solution)/shard_map/ppermute | solution.py:71
  54.7 0.6 broadcast_in_dim.102
  55.4 4.3 %all-to-all-start.1 = ((bf16[4,2,8,768]{3,2,1,0:T(8,128)(2,1)}), bf16[4,2,8,768]{3,2,1,0:T(8,128)(2,1)S(1)}, u32[]{:S(2)}, u32[]{:S(2)}) async-start(bf16[4,2,8,768]{3,2,1,0:T(8,128)(2,1)} %broadcast_in_dim.102), calls=%async_computation.1 | async-start | bytes 196608 | tf_op jit(solution)/shard_map/all_to_all | solution.py:14
  59.7 7.0 %all-to-all-done.1 = bf16[4,2,8,768]{3,2,1,0:T(8,128)(2,1)S(1)} async-done(((bf16[4,2,8,768]{3,2,1,0:T(8,128)(2,1)}), bf16[4,2,8,768]{3,2,1,0:T(8,128)(2,1)S(1)}, u32[]{:S(2)}, u32[]{:S(2)}) %all-to-all-start.1) | async-done | bytes 98336 | tf_op jit(solution)/shard_map/all_to_all | solution.py:14
  66.8 1.1 fusion.20
  67.9 5.9 %all-gather.2.cloned.1.call-done = bf16[3,1024,768]{2,1,0:T(8,128)(2,1)} async-done(((bf16[3,256,768]{2,1,0:T(8,128)(2,1)}), bf16[3,1024,768]{2,1,0:T(8,128)(2,1)}) %all-gather.2.cloned.1.call-update) | async-done | bytes 4718608 | tf_op jit(solution)/shard_map/all_gather | solution.py:58
  73.7 4.2 %fusion.3 = bf16[3,256,768]{2,1,0:T(8,128)(2,1)S(1)} fusion(bf16[3,1024,768]{2,1,0:T(8,128)(2,1)} %all-gather.2.cloned.1.call-done, bf16[3,256,1024]{2,1,0:T(8,128)(2,1)} %param.11, pred[3,1024]{1,0:T(4,128)(4,1)S(1)} %iota_compare_fusion), kind=kOutput, calls=%fused_computation.5 | convolution fusion | flops 1209335808 | bytes 7474176 | tf_op jit(solution)/shard_map/sfg,sgn->sfn/dot_general | solution.py:61
  78.0 0.5 fusion.13
  78.5 0.4 fusion.9
  79.1 0.7 pad_maximum_fusion
  79.8 3.4 %all-to-all-start.2 = ((bf16[8,2,8,768]{3,2,1,0:T(8,128)(2,1)}), bf16[8,2,8,768]{3,2,1,0:T(8,128)(2,1)S(1)}, u32[]{:S(2)}, u32[]{:S(2)}) async-start(bf16[8,2,8,768]{3,2,1,0:T(8,128)(2,1)} %bitcast.20), calls=%async_computation.2 | async-start | bytes 393216 | tf_op jit(solution)/shard_map/all_to_all | solution.py:105
  83.2 6.2 %all-to-all-done.2 = bf16[8,2,8,768]{3,2,1,0:T(8,128)(2,1)S(1)} async-done(((bf16[8,2,8,768]{3,2,1,0:T(8,128)(2,1)}), bf16[8,2,8,768]{3,2,1,0:T(8,128)(2,1)S(1)}, u32[]{:S(2)}, u32[]{:S(2)}) %all-to-all-start.2) | async-done | bytes 196640 | tf_op jit(solution)/shard_map/all_to_all | solution.py:105
  89.6 1.3 add_convert_fusion
  90.8 13.4 %all-to-all-start.3 = ((bf16[64,8,768]{2,1,0:T(8,128)(2,1)}), bf16[64,8,768]{2,1,0:T(8,128)(2,1)S(1)}, u32[]{:S(2)}, u32[]{:S(2)}) async-start(bf16[64,8,768]{2,1,0:T(8,128)(2,1)} %add_convert_fusion), calls=%async_computation.3 | async-start | bytes 1572864 | tf_op jit(solution)/shard_map/all_to_all | solution.py:120
  104.2 0.2 rev.3
  104.6 23.9 %all-to-all-done.3 = bf16[64,8,768]{2,1,0:T(8,128)(2,1)S(1)} async-done(((bf16[64,8,768]{2,1,0:T(8,128)(2,1)}), bf16[64,8,768]{2,1,0:T(8,128)(2,1)S(1)}, u32[]{:S(2)}, u32[]{:S(2)}) %all-to-all-start.3) | async-done | bytes 786464 | tf_op jit(solution)/shard_map/all_to_all | solution.py:120
  128.6 0.7 fusion.24
  (47 shorter events, 0.7 us)
Async XLA Ops:
  7.2 59.6 %copy-start = (bf16[3,192,768]{2,1,0:T(8,128)(2,1)S(1)}, bf16[3,192,768]{2,1,0:T(8,128)(2,1)}, u32[]{:S(2)}) copy-start(bf16[3,192,768]{2,1,0:T(8,128)(2,1)} %param.13) | copy-start | bytes 2654212
  7.2 19.0 %copy-start.10 = (s32[3,1]{0,1:T(1,128)S(1)}, s32[3,1]{0,1:T(1,128)}, u32[]{:S(2)}) copy-start(s32[3,1]{0,1:T(1,128)} %param.10) | copy-start | bytes 40
  7.2 21.5 %copy-start.9 = (s32[3]{0:T(128)S(1)}, s32[3]{0:T(128)}, u32[]{:S(2)}) copy-start(s32[3]{0:T(128)} %param.9) | copy-start | bytes 40
  7.2 66.5 %all-gather.2.cloned.1.call-start = ((), (), s32[]{:S(2)}) async-start(), calls=%async_computation.4 | async-start | bytes 5898240 | tf_op jit(solution)/shard_map/all_gather | solution.py:58
  9.6 40.6 %all-to-all-start = ((bf16[64,8,768]{2,1,0:T(8,128)(2,1)}), bf16[64,8,768]{2,1,0:T(8,128)(2,1)S(1)}, u32[]{:S(2)}, u32[]{:S(2)}) async-start(bf16[64,8,768]{2,1,0:T(8,128)(2,1)} %broadcast_in_dim.101), calls=%async_computation | async-start | bytes 1572864 | tf_op jit(solution)/shard_map/all_to_all | solution.py:14
  26.8 3.1 %collective-permute-start = (s32[1]{0:T(128)}, s32[1]{0:T(128)}, u32[]{:S(2)}, u32[]{:S(2)}) collective-permute-start(s32[1]{0:T(128)} %bitcast.3), channel_id=1, source_target_pairs={{0,4},{4,0},{1,5},{5,1},{2,6},{6,2},{3,7},{7,3},{8,12},{12,8},{9,1... | collective-permute-start | bytes 20 | tf_op jit(solution)/shard_map/ppermute | solution.py:69
  50.1 4.6 %collective-permute-start.1 = (bf16[8,768]{1,0:T(8,128)(2,1)S(1)}, bf16[8,768]{1,0:T(8,128)(2,1)S(1)}, u32[]{:S(2)}, u32[]{:S(2)}) collective-permute-start(bf16[8,768]{1,0:T(8,128)(2,1)S(1)} %get-tuple-element.4), channel_id=1, source_target_pairs={{0,4},{4,0},{1,5},{5,1},{2,6},{6,2},{3,7},{7,3},{8,12},{12,8},{9,1... | collective-permute-start | bytes 36872 | tf_op jit(solution)/shard_map/ppermute | solution.py:71
  55.4 11.4 %all-to-all-start.1 = ((bf16[4,2,8,768]{3,2,1,0:T(8,128)(2,1)}), bf16[4,2,8,768]{3,2,1,0:T(8,128)(2,1)S(1)}, u32[]{:S(2)}, u32[]{:S(2)}) async-start(bf16[4,2,8,768]{3,2,1,0:T(8,128)(2,1)} %broadcast_in_dim.102), calls=%async_computation.1 | async-start | bytes 196608 | tf_op jit(solution)/shard_map/all_to_all | solution.py:14
  67.9 10.6 %copy-start.1 = (bf16[3,256,768]{2,1,0:T(8,128)(2,1)S(1)}, bf16[3,256,768]{2,1,0:T(8,128)(2,1)}, u32[]{:S(2)}) copy-start(bf16[3,256,768]{2,1,0:T(8,128)(2,1)} %param.12) | copy-start | bytes 3538948
  73.7 4.8 %copy-start.3 = (f32[3,32,768]{2,1,0:T(8,128)S(1)}, f32[3,32,768]{2,1,0:T(8,128)}, u32[]{:S(2)}) copy-start(f32[3,32,768]{2,1,0:T(8,128)} %fusion.20) | copy-start | bytes 884740
  78.0 1.0 copy-start.2
  78.5 1.3 copy-start.5
  79.8 9.7 %all-to-all-start.2 = ((bf16[8,2,8,768]{3,2,1,0:T(8,128)(2,1)}), bf16[8,2,8,768]{3,2,1,0:T(8,128)(2,1)S(1)}, u32[]{:S(2)}, u32[]{:S(2)}) async-start(bf16[8,2,8,768]{3,2,1,0:T(8,128)(2,1)} %bitcast.20), calls=%async_computation.2 | async-start | bytes 393216 | tf_op jit(solution)/shard_map/all_to_all | solution.py:105
  83.2 21.0 %copy-start.4 = (bf16[1,8,768]{2,1,0:T(8,128)(2,1)S(1)}, bf16[1,8,768]{2,1,0:T(8,128)(2,1)}, u32[]{:S(2)}) copy-start(bf16[1,8,768]{2,1,0:T(8,128)(2,1)} %param.14) | copy-start | bytes 36868
  89.5 15.0 %copy-start.7 = (f32[1,768]{1,0:T(1,128)S(1)}, f32[1,768]{1,0:T(1,128)}, u32[]{:S(2)}) copy-start(f32[1,768]{1,0:T(1,128)} %param.17) | copy-start | bytes 9220
  89.5 15.0 %copy-start.8 = (f32[1,768]{1,0:T(1,128)S(1)}, f32[1,768]{1,0:T(1,128)}, u32[]{:S(2)}) copy-start(f32[1,768]{1,0:T(1,128)} %param.16) | copy-start | bytes 9220
  89.6 39.0 %copy-start.6 = (f32[1,8,768]{2,1,0:T(8,128)S(1)}, f32[1,8,768]{2,1,0:T(8,128)}, u32[]{:S(2)}) copy-start(f32[1,8,768]{2,1,0:T(8,128)} %param.15) | copy-start | bytes 73732
  90.8 37.6 %all-to-all-start.3 = ((bf16[64,8,768]{2,1,0:T(8,128)(2,1)}), bf16[64,8,768]{2,1,0:T(8,128)(2,1)S(1)}, u32[]{:S(2)}, u32[]{:S(2)}) async-start(bf16[64,8,768]{2,1,0:T(8,128)(2,1)} %add_convert_fusion), calls=%async_computation.3 | async-start | bytes 1572864 | tf_op jit(solution)/shard_map/all_to_all | solution.py:120
Sparse Core Ops, SparseCore 0:
  10.1 63.5 all-gather.1
where the time goes:
time: 137 us; the launch traced here: 136 us
  waiting for transfers between devices  62.5 us (46%)
  starting transfers between devices  41.5 us (30%)
  between operations  19.6 us (14%)
  matrix products  6.18 us (5%)
  local copies, waits for them, and re-layouts  3.31 us (2%)
  other arithmetic  3.12 us (2%)
    all_to_all x2, waiting for transfers between devices, copy_for_each(): lax.all_to_all(jnp.broadcast_to(x[None], (length, *x.shape)), axis, 0, 0,...  24.7 us
    all_to_all x1, waiting for transfers between devices, body(): lax.all_to_all(dense.astype(jnp.bfloat16), PLANE, split_axis=0, concat_ax...  23.9 us
    all_to_all x2, starting transfers between devices, copy_for_each(): lax.all_to_all(jnp.broadcast_to(x[None], (length, *x.shape)), axis, 0, 0,...  20.9 us
    all_to_all x1, starting transfers between devices, body(): lax.all_to_all(dense.astype(jnp.bfloat16), PLANE, split_axis=0, concat_ax...  13.4 us
    all_to_all x1, waiting for transfers between devices, body(): lax.all_to_all(send.reshape(2 * nharm, 2, rows_q, width).astype(jnp.bfloa...  6.23 us
    all_gather x1, waiting for transfers between devices, body(): piece = lax.all_gather(coupling, 'harm', axis=1, tiled=True)  5.86 us
    dot_general x1, matrix products, body(): jnp.einsum('sfg,sgn->sfn', front_live, piece, preferred_element_type=jnp....  4.24 us
    all_to_all x1, starting transfers between devices, body(): lax.all_to_all(send.reshape(2 * nharm, 2, rows_q, width).astype(jnp.bfloa...  3.42 us
  transfers between devices with their start and end apart: 7, of which 6 were waited for; matrix products, arithmetic and copies ran while one was open for 3% of the time, Pallas kernels for 0%

commit v1 on v0

--- a/solution.py
+++ b/solution.py
@@ -55,7 +55,8 @@
     own_rows = harm_idx * front_q + jnp.arange(front_q, dtype=jnp.int32)
     live_rows = own_rows[None, :] < lengths[:, None]
     masked = jnp.where(live_rows[:, :, None], coupling, jnp.zeros_like(coupling))
-    piece = lax.all_gather(coupling, "harm", axis=1, tiled=True)
+    copies = jnp.concatenate([coupling] * lax.axis_size("harm"), axis=1)
+    piece = lax.all_to_all(copies, "harm", 1, 1, tiled=True)
     live_cols = jnp.arange(nharm * front_q, dtype=jnp.int32)[None, :] < lengths[:, None]
     front_live = jnp.where(live_cols[:, None, :], front_inverse, jnp.zeros_like(front_inverse))
     modes = jnp.einsum(

time: 137 us -> 188 us (1.37)
  waiting for transfers between devices: 62.5 us -> 120 us
  between operations: 19.6 us -> 6.45 us
  other arithmetic: 3.12 us -> 9.46 us
  local copies, waits for them, and re-layouts: 3.31 us -> 5.68 us
    all_to_all x0 -> x1, waiting for transfers between devices: none -> 71.4 us  [body(): piece = lax.all_to_all(copies, 'harm', 1, 1, tiled=True)]
    all_to_all x2, waiting for transfers between devices: 24.7 us -> 17.5 us  [copy_for_each(): lax.all_to_all(jnp.broadcast_to(x[None], (length, *x.shape)), axis, 0, 0,...]
    all_to_all x1, starting transfers between devices: 13.4 us -> 6.55 us  [body(): lax.all_to_all(dense.astype(jnp.bfloat16), PLANE, split_axis=0, concat_ax...]
    concatenate x0 -> x1, other arithmetic: none -> 6.33 us  [body(): copies = jnp.concatenate([coupling] * lax.axis_size('harm'), axis=1)]
    all_gather x1 -> x0, waiting for transfers between devices: 5.86 us -> none  [body(): piece = lax.all_gather(coupling, 'harm', axis=1, tiled=True)]
    all_to_all x0 -> x1, starting transfers between devices: none -> 5.4 us  [body(): piece = lax.all_to_all(copies, 'harm', 1, 1, tiled=True)]
    unnamed x22 -> x21, local copies, waits for them, and re-layouts: 0.16 us -> 2.45 us
  transfers between devices with their start and end apart: 7 -> 7, of which waited for: 6 -> 5; matrix products, arithmetic and copies ran while one was open for 3% -> 5% of each run, Pallas kernels for 0% -> 0%
where the time goes in v1:
time: 188 us
  waiting for transfers between devices  120 us (64%)
  starting transfers between devices  40 us (21%)
  other arithmetic  9.46 us (5%)
  between operations  6.45 us (3%)
  matrix products  5.91 us (3%)
  local copies, waits for them, and re-layouts  5.68 us (3%)
    all_to_all x1, waiting for transfers between devices, body(): piece = lax.all_to_all(copies, 'harm', 1, 1, tiled=True)  71.4 us
    all_to_all x1, waiting for transfers between devices, body(): lax.all_to_all(dense.astype(jnp.bfloat16), PLANE, split_axis=0, concat_ax...  23.9 us
    all_to_all x2, starting transfers between devices, copy_for_each(): lax.all_to_all(jnp.broadcast_to(x[None], (length, *x.shape)), axis, 0, 0,...  20.9 us
    all_to_all x2, waiting for transfers between devices, copy_for_each(): lax.all_to_all(jnp.broadcast_to(x[None], (length, *x.shape)), axis, 0, 0,...  17.5 us
    all_to_all x1, starting transfers between devices, body(): lax.all_to_all(dense.astype(jnp.bfloat16), PLANE, split_axis=0, concat_ax...  6.55 us
    concatenate x1, other arithmetic, body(): copies = jnp.concatenate([coupling] * lax.axis_size('harm'), axis=1)  6.33 us
    all_to_all x1, waiting for transfers between devices, body(): lax.all_to_all(send.reshape(2 * nharm, 2, rows_q, width).astype(jnp.bfloa...  6.15 us
    all_to_all x1, starting transfers between devices, body(): piece = lax.all_to_all(copies, 'harm', 1, 1, tiled=True)  5.4 us
  transfers between devices with their start and end apart: 7, of which 5 were waited for; matrix products, arithmetic and copies ran while one was open for 5% of the time, Pallas kernels for 0%

profile of v1, /device:TPU:8, one launch (start us, length us, event | category | flops | bytes accessed | tf_op | source)
XLA Modules:
  0.0 187.6 jit_solution(662922883978646098)
XLA Ops:
  0.7 1.7 broadcast_in_dim.101
  2.4 16.6 %all-to-all-start = ((bf16[64,8,768]{2,1,0:T(8,128)(2,1)}), bf16[64,8,768]{2,1,0:T(8,128)(2,1)S(1)}, u32[]{:S(2)}, u32[]{:S(2)}) async-start(bf16[64,8,768]{2,1,0:T(8,128)(2,1)} %broadcast_in_dim.101), calls=%async_computation | async-start | bytes 1572864 | tf_op jit(solution)/shard_map/all_to_all | solution.py:14
  19.0 0.6 slice.46
  19.6 1.9 %collective-permute-start = (s32[1]{0:T(128)}, s32[1]{0:T(128)}, u32[]{:S(2)}, u32[]{:S(2)}) collective-permute-start(s32[1]{0:T(128)} %bitcast.3), channel_id=1, source_target_pairs={{0,4},{4,0},{1,5},{5,1},{2,6},{6,2},{3,7},{7,3},{8,12},{12,8},{9,1... | collective-permute-start | bytes 20 | tf_op jit(solution)/shard_map/ppermute | solution.py:70
  21.5 1.2 collective-permute-done
  25.5 17.5 %all-to-all-done = bf16[64,8,768]{2,1,0:T(8,128)(2,1)S(1)} async-done(((bf16[64,8,768]{2,1,0:T(8,128)(2,1)}), bf16[64,8,768]{2,1,0:T(8,128)(2,1)S(1)}, u32[]{:S(2)}, u32[]{:S(2)}) %all-to-all-start) | async-done | bytes 786464 | tf_op jit(solution)/shard_map/all_to_all | solution.py:14
  42.9 1.9 %collective-permute-start.1 = (bf16[8,768]{1,0:T(8,128)(2,1)S(1)}, bf16[8,768]{1,0:T(8,128)(2,1)S(1)}, u32[]{:S(2)}, u32[]{:S(2)}) collective-permute-start(bf16[8,768]{1,0:T(8,128)(2,1)S(1)} %get-tuple-element.4), channel_id=1, source_target_pairs={{0,4},{4,0},{1,5},{5,1},{2,6},{6,2},{3,7},{7,3},{8,12},{12,8},{9,1... | collective-permute-start | bytes 36872 | tf_op jit(solution)/shard_map/ppermute | solution.py:72
  47.5 2.3 %copy.25 = bf16[3,256,768]{2,0,1:T(4,128)(2,1)S(1)} copy(bf16[3,256,768]{2,1,0:T(8,128)(2,1)} %param.12) | data formatting | bytes 2359296 | tf_op args[3]
  49.8 0.6 broadcast_in_dim.102
  50.5 4.3 %all-to-all-start.1 = ((bf16[4,2,8,768]{3,2,1,0:T(8,128)(2,1)}), bf16[4,2,8,768]{3,2,1,0:T(8,128)(2,1)S(1)}, u32[]{:S(2)}, u32[]{:S(2)}) async-start(bf16[4,2,8,768]{3,2,1,0:T(8,128)(2,1)} %broadcast_in_dim.102), calls=%async_computation.1 | async-start | bytes 196608 | tf_op jit(solution)/shard_map/all_to_all | solution.py:14
  54.8 6.3 %pad_maximum_fusion = bf16[3,1024,768]{2,0,1:T(4,128)(2,1)} fusion(bf16[3,256,768]{2,0,1:T(4,128)(2,1)S(1)} %copy.25), kind=kLoop, calls=%fused_computation | loop fusion | flops 7077888 | bytes 5898240 | tf_op jit(solution)/shard_map/concatenate | solution.py:58
  61.1 5.4 %all-to-all-start.2 = ((bf16[3,1024,768]{2,0,1:T(4,128)(2,1)}), bf16[3,1024,768]{2,0,1:T(4,128)(2,1)}, u32[]{:S(2)}, u32[]{:S(2)}) async-start(bf16[3,1024,768]{2,0,1:T(4,128)(2,1)} %pad_maximum_fusion), calls=%async_computation.2 | async-start | bytes 12582912 | tf_op jit(solution)/shard_map/all_to_all | solution.py:59
  66.7 0.3 fusion.23
  67.1 71.4 %all-to-all-done.2 = bf16[3,1024,768]{2,0,1:T(4,128)(2,1)} async-done(((bf16[3,1024,768]{2,0,1:T(4,128)(2,1)}), bf16[3,1024,768]{2,0,1:T(4,128)(2,1)}, u32[]{:S(2)}, u32[]{:S(2)}) %all-to-all-start.2) | async-done | bytes 4718624 | tf_op jit(solution)/shard_map/all_to_all | solution.py:59
  138.5 4.7 %fusion.4 = bf16[3,256,768]{2,1,0:T(8,128)(2,1)S(1)} fusion(bf16[3,1024,768]{2,0,1:T(4,128)(2,1)} %all-to-all-done.2, bf16[3,256,1024]{2,1,0:T(8,128)(2,1)} %param.11, pred[3,1024]{1,0:T(4,128)(4,1)S(1)} %iota_compare_fusion), kind=kOutput, calls=%fused_computation.7 | convolution fusion | flops 1209335808 | bytes 7474176 | tf_op jit(solution)/shard_map/sfg,sgn->sfn/dot_general | solution.py:62
  143.2 0.5 fusion.16
  143.7 0.4 fusion.12
  144.3 0.7 pad_maximum_fusion.1
  145.0 3.4 %all-to-all-start.3 = ((bf16[8,2,8,768]{3,2,1,0:T(8,128)(2,1)}), bf16[8,2,8,768]{3,2,1,0:T(8,128)(2,1)S(1)}, u32[]{:S(2)}, u32[]{:S(2)}) async-start(bf16[8,2,8,768]{3,2,1,0:T(8,128)(2,1)} %bitcast.20), calls=%async_computation.3 | async-start | bytes 393216 | tf_op jit(solution)/shard_map/all_to_all | solution.py:106
  148.4 6.1 %all-to-all-done.3 = bf16[8,2,8,768]{3,2,1,0:T(8,128)(2,1)S(1)} async-done(((bf16[8,2,8,768]{3,2,1,0:T(8,128)(2,1)}), bf16[8,2,8,768]{3,2,1,0:T(8,128)(2,1)S(1)}, u32[]{:S(2)}, u32[]{:S(2)}) %all-to-all-start.3) | async-done | bytes 196640 | tf_op jit(solution)/shard_map/all_to_all | solution.py:106
  154.7 1.3 add_convert_fusion
  155.9 6.6 %all-to-all-start.4 = ((bf16[64,8,768]{2,1,0:T(8,128)(2,1)}), bf16[64,8,768]{2,1,0:T(8,128)(2,1)S(1)}, u32[]{:S(2)}, u32[]{:S(2)}) async-start(bf16[64,8,768]{2,1,0:T(8,128)(2,1)} %add_convert_fusion), calls=%async_computation.4 | async-start | bytes 1572864 | tf_op jit(solution)/shard_map/all_to_all | solution.py:121
  162.9 23.9 %all-to-all-done.4 = bf16[64,8,768]{2,1,0:T(8,128)(2,1)S(1)} async-done(((bf16[64,8,768]{2,1,0:T(8,128)(2,1)}), bf16[64,8,768]{2,1,0:T(8,128)(2,1)S(1)}, u32[]{:S(2)}, u32[]{:S(2)}) %all-to-all-start.4) | async-done | bytes 786464 | tf_op jit(solution)/shard_map/all_to_all | solution.py:121
  186.9 0.7 fusion.27
  (46 shorter events, 0.9 us)
Async XLA Ops:
  0.6 66.1 %copy-start = (bf16[3,192,768]{2,1,0:T(8,128)(2,1)S(1)}, bf16[3,192,768]{2,1,0:T(8,128)(2,1)}, u32[]{:S(2)}) copy-start(bf16[3,192,768]{2,1,0:T(8,128)(2,1)} %param.13) | copy-start | bytes 2654212
  0.6 18.3 %copy-start.9 = (s32[3,1]{0,1:T(1,128)S(1)}, s32[3,1]{0,1:T(1,128)}, u32[]{:S(2)}) copy-start(s32[3,1]{0,1:T(1,128)} %param.10) | copy-start | bytes 40
  2.4 40.6 %all-to-all-start = ((bf16[64,8,768]{2,1,0:T(8,128)(2,1)}), bf16[64,8,768]{2,1,0:T(8,128)(2,1)S(1)}, u32[]{:S(2)}, u32[]{:S(2)}) async-start(bf16[64,8,768]{2,1,0:T(8,128)(2,1)} %broadcast_in_dim.101), calls=%async_computation | async-start | bytes 1572864 | tf_op jit(solution)/shard_map/all_to_all | solution.py:14
  19.6 3.1 %collective-permute-start = (s32[1]{0:T(128)}, s32[1]{0:T(128)}, u32[]{:S(2)}, u32[]{:S(2)}) collective-permute-start(s32[1]{0:T(128)} %bitcast.3), channel_id=1, source_target_pairs={{0,4},{4,0},{1,5},{5,1},{2,6},{6,2},{3,7},{7,3},{8,12},{12,8},{9,1... | collective-permute-start | bytes 20 | tf_op jit(solution)/shard_map/ppermute | solution.py:70
  42.9 6.8 %collective-permute-start.1 = (bf16[8,768]{1,0:T(8,128)(2,1)S(1)}, bf16[8,768]{1,0:T(8,128)(2,1)S(1)}, u32[]{:S(2)}, u32[]{:S(2)}) collective-permute-start(bf16[8,768]{1,0:T(8,128)(2,1)S(1)} %get-tuple-element.4), channel_id=1, source_target_pairs={{0,4},{4,0},{1,5},{5,1},{2,6},{6,2},{3,7},{7,3},{8,12},{12,8},{9,1... | collective-permute-start | bytes 36872 | tf_op jit(solution)/shard_map/ppermute | solution.py:72
  50.5 10.6 %all-to-all-start.1 = ((bf16[4,2,8,768]{3,2,1,0:T(8,128)(2,1)}), bf16[4,2,8,768]{3,2,1,0:T(8,128)(2,1)S(1)}, u32[]{:S(2)}, u32[]{:S(2)}) async-start(bf16[4,2,8,768]{3,2,1,0:T(8,128)(2,1)} %broadcast_in_dim.102), calls=%async_computation.1 | async-start | bytes 196608 | tf_op jit(solution)/shard_map/all_to_all | solution.py:14
  61.1 5.4 %copy-start.8 = (s32[3]{0:T(128)S(1)}, s32[3]{0:T(128)}, u32[]{:S(2)}) copy-start(s32[3]{0:T(128)} %param.9) | copy-start | bytes 40
  61.1 77.4 %all-to-all-start.2 = ((bf16[3,1024,768]{2,0,1:T(4,128)(2,1)}), bf16[3,1024,768]{2,0,1:T(4,128)(2,1)}, u32[]{:S(2)}, u32[]{:S(2)}) async-start(bf16[3,1024,768]{2,0,1:T(4,128)(2,1)} %pad_maximum_fusion), calls=%async_computation.2 | async-start | bytes 12582912 | tf_op jit(solution)/shard_map/all_to_all | solution.py:59
  67.1 76.6 %copy-start.2 = (bf16[3,256,768]{2,1,0:T(8,128)(2,1)S(1)}, bf16[3,256,768]{2,1,0:T(8,128)(2,1)}, u32[]{:S(2)}) copy-start(bf16[3,256,768]{2,1,0:T(8,128)(2,1)} %param.12) | copy-start | bytes 3538948
  143.2 1.0 copy-start.1
  143.7 1.3 copy-start.4
  145.0 9.6 %all-to-all-start.3 = ((bf16[8,2,8,768]{3,2,1,0:T(8,128)(2,1)}), bf16[8,2,8,768]{3,2,1,0:T(8,128)(2,1)S(1)}, u32[]{:S(2)}, u32[]{:S(2)}) async-start(bf16[8,2,8,768]{3,2,1,0:T(8,128)(2,1)} %bitcast.20), calls=%async_computation.3 | async-start | bytes 393216 | tf_op jit(solution)/shard_map/all_to_all | solution.py:106
  148.4 14.1 %copy-start.3 = (bf16[1,8,768]{2,1,0:T(8,128)(2,1)S(1)}, bf16[1,8,768]{2,1,0:T(8,128)(2,1)}, u32[]{:S(2)}) copy-start(bf16[1,8,768]{2,1,0:T(8,128)(2,1)} %param.14) | copy-start | bytes 36868
  154.6 8.2 %copy-start.6 = (f32[1,768]{1,0:T(1,128)S(1)}, f32[1,768]{1,0:T(1,128)}, u32[]{:S(2)}) copy-start(f32[1,768]{1,0:T(1,128)} %param.17) | copy-start | bytes 9220
  154.6 8.2 %copy-start.7 = (f32[1,768]{1,0:T(1,128)S(1)}, f32[1,768]{1,0:T(1,128)}, u32[]{:S(2)}) copy-start(f32[1,768]{1,0:T(1,128)} %param.16) | copy-start | bytes 9220
  154.7 32.2 %copy-start.5 = (f32[1,8,768]{2,1,0:T(8,128)S(1)}, f32[1,8,768]{2,1,0:T(8,128)}, u32[]{:S(2)}) copy-start(f32[1,8,768]{2,1,0:T(8,128)} %param.15) | copy-start | bytes 73732
  155.9 30.8 %all-to-all-start.4 = ((bf16[64,8,768]{2,1,0:T(8,128)(2,1)}), bf16[64,8,768]{2,1,0:T(8,128)(2,1)S(1)}, u32[]{:S(2)}, u32[]{:S(2)}) async-start(bf16[64,8,768]{2,1,0:T(8,128)(2,1)} %add_convert_fusion), calls=%async_computation.4 | async-start | bytes 1572864 | tf_op jit(solution)/shard_map/all_to_all | solution.py:121
